TPU v7x, 512 devices: a whole 4x8x8 slice. The times are simulated.
512 devices in a mesh: section: 8 (over y), dp: 64 (over x, z, core).
Axes of the slice: x: 4, y: 8, z: 8, core: 2. Of those that a mesh axis runs over, the one named last changes fastest.
Arguments:
- queries: bfloat16 [65536, 3584], P(('section', 'dp')), may hold values from -1 to 1
- passages: bfloat16 [128, 64, 3584], P('dp'), may hold values from -1 to 1
- candidates: int32 [512, 3], P('section'), may hold values from 0 to 63, as said below
- counts: int32 [512], P('section'), may hold values from 1 to 3, 1024 in all
- teacher: float32 [65536, 384], P(('section', 'dp')), may hold values from -20 to 450
- section_weights: bfloat16 [8, 3584, 3584], P('section', 'dp'), may hold values from -0.09375 to 0.09375
- section_inputs: bfloat16 [8, 64, 3584], P('section', None, 'dp'), may hold values from -1.5 to 1.5
- pre_acts: bfloat16 [8, 64, 3584], P('section', None, 'dp'), may hold values from -8 to 8
Outputs:
- query_grads: bfloat16 [65536, 3584], P(('section', 'dp'))
- passage_grads: bfloat16 [128, 64, 3584], P('dp')
- grad_inputs: float32 [8, 64, 3584], P('section', None, 'dp')
- weight_grads: bfloat16 [8, 3584, 3584], P('section', 'dp')
Inputs may be any that keep to these rules, and one draw needn't show every extreme that they name: `candidates`: each row names 3 different passage blocks. A query block uses the first counts[b] entries of its row of candidates.
All inputs are finite; a program needn't handle non-finite values.
Results may differ from a plain program's by a relative error of at most 0.0085.
Values may be sent and summed in bfloat16 or wider, within the bound.
No kernel may reach another device: no remote copies, remote signals or barrier semaphores. Data moves between devices by JAX's collectives and lax.ppermute only.
A program may use at most 64 MiB of HBM per device.

v0:
```python
import jax
import jax.numpy as jnp
from jax import lax
from jax.sharding import PartitionSpec as P

INVERSE_TEMP = 20.0


def passed_along(value, axis, steps):
    count = lax.axis_size(axis)
    initial, last = (max(0, -steps), min(count, count - steps))
    return lax.ppermute(value, axis, [(source, source + steps) for source in range(initial, last)])


def soft_weights(logits, valid):
    masked = jnp.where(valid, logits, -1e30)
    highest = jnp.max(masked, axis=-1, keepdims=True)
    expons = jnp.where(valid, jnp.exp(masked - highest), 0.0)
    return expons / jnp.sum(expons, axis=-1, keepdims=True)


def body(queries, passages, candidates, counts, teacher, section_weights, section_inputs, pre_acts):
    dp_count = lax.axis_size("dp")
    dp_index = lax.axis_index("dp")
    stripe, block_total, width = passages.shape
    row_block_count = stripe * dp_count
    blocks_here = candidates.shape[0] // dp_count
    slot_count = candidates.shape[1]
    requests = blocks_here * slot_count
    all_slots = candidates.reshape(-1)
    outgoing = jnp.take(passages, all_slots, axis=1)
    pulled_rows = lax.all_to_all(outgoing, "dp", split_axis=1, concat_axis=0, tiled=True)
    pulled_rows = pulled_rows.reshape(row_block_count, blocks_here, slot_count, width)
    own_counts = lax.dynamic_slice_in_dim(counts, dp_index * blocks_here, blocks_here)
    slot_valid = jnp.arange(slot_count, dtype=jnp.int32)[None, :] < own_counts[:, None]
    column_valid = jnp.repeat(slot_valid, row_block_count, axis=1)[:, None, :]
    query_row_items = queries.reshape(blocks_here, row_block_count, width)
    logits = (
        jnp.einsum(
            "ixp,wifp->ixfw", query_row_items, pulled_rows, preferred_element_type=jnp.float32
        )
        * INVERSE_TEMP
    )
    logits = logits.reshape(blocks_here, row_block_count, slot_count * row_block_count)
    target_logits = soft_weights(
        teacher.reshape(blocks_here, row_block_count, slot_count * row_block_count), column_valid
    )
    weight_matrices = (soft_weights(logits, column_valid) - target_logits).astype(jnp.bfloat16)
    weight_matrices = weight_matrices.reshape(
        blocks_here, row_block_count, slot_count, row_block_count
    )
    query_sums = (
        jnp.einsum(
            "geal,lgay->gey", weight_matrices, pulled_rows, preferred_element_type=jnp.float32
        )
        * INVERSE_TEMP
    )
    passage_sums = (
        jnp.einsum(
            "fnyw,fnj->wfyj", weight_matrices, query_row_items, preferred_element_type=jnp.float32
        )
        * INVERSE_TEMP
    )
    block_terms = passage_sums.reshape(row_block_count, requests, width).astype(jnp.bfloat16)
    micro_count = section_inputs.shape[1] // dp_count
    col_width = width // dp_count
    micro_cols = jnp.transpose(
        query_sums[0, :micro_count].reshape(micro_count, dp_count, col_width), (1, 0, 2)
    )
    incoming_piece = lax.all_to_all(block_terms, "dp", split_axis=0, concat_axis=1, tiled=True)
    entry = lax.all_to_all(micro_cols, "dp", split_axis=0, concat_axis=1, tiled=True)
    onehot = (all_slots[:, None] == jnp.arange(block_total, dtype=jnp.int32)[None, :]).astype(
        jnp.float32
    )
    dense = jnp.einsum(
        "sjd,jn->snd",
        incoming_piece.astype(jnp.float32),
        onehot,
        precision=lax.Precision.HIGHEST,
        preferred_element_type=jnp.float32,
    )
    passage_out = lax.psum(dense, "section").astype(jnp.bfloat16)
    weight_rows = section_weights[0]
    input_cols = section_inputs[0]
    pre = pre_acts[0].astype(jnp.float32)
    sigma = jax.nn.sigmoid(pre)
    slope = sigma * (1.0 + pre * (1.0 - sigma))
    carry = entry.reshape(dp_count * micro_count, col_width)
    section_count = lax.axis_size("section")
    section_index = lax.axis_index("section")
    grad_cols = jnp.zeros_like(carry)
    grad_weight = jnp.zeros((col_width, width), jnp.float32)
    for section_turn in range(section_count):
        active_flag = section_count - 1 - section_turn
        inner = (carry * slope).astype(jnp.bfloat16)
        piece = lax.all_gather(inner, "dp", axis=1, tiled=True)
        back_sum = jnp.einsum("mj,ij->mi", piece, weight_rows, preferred_element_type=jnp.float32)
        weight_part = jnp.einsum("mi,mj->ij", input_cols, piece, preferred_element_type=jnp.float32)
        back_sum, layer_weight = (back_sum, weight_part)
        updated = carry + back_sum
        is_active = section_index == active_flag
        grad_cols = jnp.where(is_active, updated, grad_cols)
        grad_weight = jnp.where(is_active, layer_weight, grad_weight)
        if section_turn + 1 < section_count:
            carry = passed_along(updated, "section", -1)
    return (
        query_sums.reshape(blocks_here * row_block_count, width).astype(jnp.bfloat16),
        passage_out,
        grad_cols[None],
        grad_weight[None].astype(jnp.bfloat16),
    )


def solution(mesh):
    placed = (
        P(("section", "dp"), None),
        P("dp", None, None),
        P("section", None),
        P("section"),
        P(("section", "dp"), None),
        P("section", "dp", None),
        P("section", None, "dp"),
        P("section", None, "dp"),
    )
    return jax.shard_map(
        body,
        mesh=mesh,
        in_specs=placed,
        out_specs=(
            P(("section", "dp"), None),
            P("dp", None, None),
            P("section", None, "dp"),
            P("section", "dp", None),
        ),
        check_vma=False,
    )
```

profile of v0, /device:TPU:16, one launch (start us, length us, event | category | flops | bytes accessed | tf_op | source)
XLA Modules:
  0.0 732.7 jit_solution(10540011991136659404)
XLA Ops:
  0.6 0.9 copy.27
  1.6 0.1 reshape.238
  1.8 15.2 %gather_fusion = bf16[192,2,3584]{2,0,1:T(8,128)(2,1)} fusion(bf16[2,64,3584]{2,1,0:T(8,128)(2,1)} %param.9, s32[1024]{0:T(1024)S(1)} %pad_clamp_fusion), kind=kCustom, calls=%fused_computation | custom fusion | bytes 5505792 | tf_op jit(solution)/shard_map/jit(_take)/gather | solution.py:31
  17.0 2.1 select_bitcast_fusion
  19.1 4.4 copy.29
  23.5 14.1 %all-to-all-start = ((bf16[2,192,3584]{2,0,1:T(2,128)(2,1)}), bf16[2,192,3584]{2,0,1:T(2,128)(2,1)}, u32[]{:S(2)}, u32[]{:S(2)}) async-start(bf16[2,192,3584]{2,0,1:T(2,128)(2,1)} %copy.29), calls=%async_computation | async-start | bytes 5505024 | tf_op jit(solution)/shard_map/all_to_all | solution.py:32
  37.8 0.6 dynamic_slice.3
  38.4 0.6 iota_compare_fusion.1
  39.2 0.1 select_reduce_fusion
  39.3 0.1 fusion.29
  39.5 62.7 %all-to-all-done = bf16[2,192,3584]{2,0,1:T(2,128)(2,1)} async-done(((bf16[2,192,3584]{2,0,1:T(2,128)(2,1)}), bf16[2,192,3584]{2,0,1:T(2,128)(2,1)}, u32[]{:S(2)}, u32[]{:S(2)}) %all-to-all-start) | async-done | bytes 2752544 | tf_op jit(solution)/shard_map/all_to_all | solution.py:32
  102.2 5.2 copy.30
  107.4 6.8 reshape.239
  114.2 2.8 fusion.27
  117.0 0.1 fusion.21
  117.2 0.2 fusion.28
  117.4 1.6 fusion.47
  119.0 0.7 transpose_reshape_squeeze.3
  119.7 6.2 all-to-all-start.2
  125.9 0.9 fusion.1
  126.7 4.2 copy.33
  131.0 4.3 all-to-all-done.2
  135.3 6.4 all-to-all-start.1
  141.8 124.8 %all_gather.24 = bf16[64,3584]{0,1:T(8,128)(2,1)S(1)} all-gather(bf16[64,56]{0,1:T(8,128)(2,1)S(1)} %fusion.38), channel_id=1, replica_groups=mesh['section'=8,'dp'=64] {'dp'}, dimensions={1}, use_global_device_ids=true | all-gather | bytes 465920 | tf_op jit(solution)/shard_map/all_gather | solution.py:96
  266.6 0.3 convolution_add_fusion.7
  266.9 2.8 collective-permute-start
  269.7 0.7 convolution_select_fusion
  270.4 2.3 collective-permute-done
  272.7 49.7 %all_gather.25 = bf16[64,3584]{0,1:T(8,128)(2,1)S(1)} all-gather(bf16[64,56]{0,1:T(8,128)(2,1)S(1)} %multiply_convert_fusion.6), channel_id=1, replica_groups=mesh['section'=8,'dp'=64] {'dp'}, dimensions={1}, use_global_device_ids=true | all-gather | bytes 465920 | tf_op jit(solution)/shard_map/all_gather | solution.py:96
  322.4 0.3 convolution_add_fusion.6
  322.7 2.8 collective-permute-start.1
  325.5 0.7 convolution_select_fusion.1
  326.2 2.9 collective-permute-done.1
  329.1 48.2 %all_gather.26 = bf16[64,3584]{0,1:T(8,128)(2,1)S(1)} all-gather(bf16[64,56]{0,1:T(8,128)(2,1)S(1)} %multiply_convert_fusion.5), channel_id=1, replica_groups=mesh['section'=8,'dp'=64] {'dp'}, dimensions={1}, use_global_device_ids=true | all-gather | bytes 465920 | tf_op jit(solution)/shard_map/all_gather | solution.py:96
  377.3 0.3 convolution_add_fusion.5
  377.6 2.2 collective-permute-start.2
  379.8 0.7 convolution_select_fusion.2
  380.5 4.1 collective-permute-done.2
  384.6 50.1 %all_gather.27 = bf16[64,3584]{0,1:T(8,128)(2,1)S(1)} all-gather(bf16[64,56]{0,1:T(8,128)(2,1)S(1)} %multiply_convert_fusion.4), channel_id=1, replica_groups=mesh['section'=8,'dp'=64] {'dp'}, dimensions={1}, use_global_device_ids=true | all-gather | bytes 465920 | tf_op jit(solution)/shard_map/all_gather | solution.py:96
  434.7 0.3 convolution_add_fusion.4
  435.0 1.9 collective-permute-start.3
  436.9 0.7 convolution_select_fusion.3
  437.6 4.4 collective-permute-done.3
  442.0 48.2 %all_gather.28 = bf16[64,3584]{0,1:T(8,128)(2,1)S(1)} all-gather(bf16[64,56]{0,1:T(8,128)(2,1)S(1)} %multiply_convert_fusion.3), channel_id=1, replica_groups=mesh['section'=8,'dp'=64] {'dp'}, dimensions={1}, use_global_device_ids=true | all-gather | bytes 465920 | tf_op jit(solution)/shard_map/all_gather | solution.py:96
  490.2 0.3 convolution_add_fusion.3
  490.5 1.9 collective-permute-start.4
  492.4 0.7 convolution_select_fusion.4
  493.1 4.4 collective-permute-done.4
  497.5 49.7 %all_gather.29 = bf16[64,3584]{0,1:T(8,128)(2,1)S(1)} all-gather(bf16[64,56]{0,1:T(8,128)(2,1)S(1)} %multiply_convert_fusion.2), channel_id=1, replica_groups=mesh['section'=8,'dp'=64] {'dp'}, dimensions={1}, use_global_device_ids=true | all-gather | bytes 465920 | tf_op jit(solution)/shard_map/all_gather | solution.py:96
  547.2 0.3 convolution_add_fusion.2
  547.4 1.9 collective-permute-start.5
  549.4 0.7 convolution_select_fusion.5
  550.0 4.4 collective-permute-done.5
  554.5 48.3 %all_gather.30 = bf16[64,3584]{0,1:T(8,128)(2,1)S(1)} all-gather(bf16[64,56]{0,1:T(8,128)(2,1)S(1)} %multiply_convert_fusion.1), channel_id=1, replica_groups=mesh['section'=8,'dp'=64] {'dp'}, dimensions={1}, use_global_device_ids=true | all-gather | bytes 465920 | tf_op jit(solution)/shard_map/all_gather | solution.py:96
  602.8 0.3 convolution_add_fusion.1
  603.1 1.9 collective-permute-start.6
  605.0 0.7 convolution_select_fusion.6
  605.7 4.4 collective-permute-done.6
  610.1 49.7 %all_gather.31 = bf16[64,3584]{0,1:T(8,128)(2,1)S(1)} all-gather(bf16[64,56]{0,1:T(8,128)(2,1)S(1)} %multiply_convert_fusion), channel_id=1, replica_groups=mesh['section'=8,'dp'=64] {'dp'}, dimensions={1}, use_global_device_ids=true | all-gather | bytes 465920 | tf_op jit(solution)/shard_map/all_gather | solution.py:96
  659.8 1.4 fusion.4
  661.2 0.9 fusion.7
  662.1 4.4 copy.34
  666.5 0.6 convolution_bitcast_fusion
  667.1 65.4 %all-reduce.1 = bf16[2,64,3584]{2,1,0:T(8,128)(2,1)} all-reduce(f32[2,64,3584]{2,1,0:T(8,128)S(1)} %convolution_bitcast_fusion), channel_id=1, replica_groups=mesh['section'=8,'dp'=64] {'section'}, use_global_device_ids=true, to_apply=%region_4.5 | all-reduce | flops 458752 | bytes 2752512 | tf_op jit(solution)/shard_map/psum | solution.py:82
  (31 shorter events, 0.7 us)
Async XLA Ops:
  0.6 113.6 %copy-start = (bf16[128,3584]{1,0:T(8,128)(2,1)S(1)}, bf16[128,3584]{1,0:T(8,128)(2,1)}, u32[]{:S(2)}) copy-start(bf16[128,3584]{1,0:T(8,128)(2,1)} %param.8) | copy-start | bytes 2752516
  23.5 14.2 %copy-start.5 = (f32[128,384]{1,0:T(8,128)S(1)}, f32[128,384]{1,0:T(8,128)}, u32[]{:S(2)}) copy-start(f32[128,384]{1,0:T(8,128)} %param.12) | copy-start | bytes 589828
  23.5 14.3 %copy-start.6 = (s32[64]{0:T(128)S(1)}, s32[64]{0:T(128)}, u32[]{:S(2)}) copy-start(s32[64]{0:T(128)} %param.11) | copy-start | bytes 772
  23.5 78.7 %all-to-all-start = ((bf16[2,192,3584]{2,0,1:T(2,128)(2,1)}), bf16[2,192,3584]{2,0,1:T(2,128)(2,1)}, u32[]{:S(2)}, u32[]{:S(2)}) async-start(bf16[2,192,3584]{2,0,1:T(2,128)(2,1)} %copy.29), calls=%async_computation | async-start | bytes 5505024 | tf_op jit(solution)/shard_map/all_to_all | solution.py:32
  114.2 3.1 copy-start.1
  119.7 15.6 %all-to-all-start.2 = ((f32[64,1,56]{2,1,0:T(1,128)}), f32[64,1,56]{2,1,0:T(1,128)S(1)}, u32[]{:S(2)}, u32[]{:S(2)}) async-start(f32[64,1,56]{2,1,0:T(1,128)} %bitcast.24), calls=%async_computation.2 | async-start | bytes 65536 | tf_op jit(solution)/shard_map/all_to_all | solution.py:71
  131.0 10.8 %copy-start.4 = (bf16[1,64,56]{1,2,0:T(8,128)(2,1)S(1)}, bf16[1,64,56]{1,2,0:T(8,128)(2,1)}, u32[]{:S(2)}) copy-start(bf16[1,64,56]{1,2,0:T(8,128)(2,1)} %param.15) | copy-start | bytes 21508
  131.0 135.7 %copy-start.2 = (bf16[1,56,3584]{2,1,0:T(8,128)(2,1)S(1)}, bf16[1,56,3584]{2,1,0:T(8,128)(2,1)}, u32[]{:S(2)}) copy-start(bf16[1,56,3584]{2,1,0:T(8,128)(2,1)} %param.13) | copy-start | bytes 1204228
  131.0 138.8 %copy-start.3 = (bf16[1,64,56]{1,2,0:T(8,128)(2,1)S(1)}, bf16[1,64,56]{1,2,0:T(8,128)(2,1)}, u32[]{:S(2)}) copy-start(bf16[1,64,56]{1,2,0:T(8,128)(2,1)} %param.14) | copy-start | bytes 21508
  135.3 526.8 %all-to-all-start.1 = ((bf16[128,3,3584]{2,1,0:T(4,128)(2,1)}), bf16[128,3,3584]{2,1,0:T(4,128)(2,1)}, u32[]{:S(2)}, u32[]{:S(2)}) async-start(bf16[128,3,3584]{2,1,0:T(4,128)(2,1)} %copy.33), calls=%async_computation.1 | async-start | bytes 7340032 | tf_op jit(solution)/shard_map/all_to_all | solution.py:70
  266.9 5.8 collective-permute-start
  322.7 6.4 collective-permute-start.1
  377.6 7.0 collective-permute-start.2
  435.0 7.0 collective-permute-start.3
  490.5 7.0 collective-permute-start.4
  547.4 7.0 collective-permute-start.5
  603.1 7.0 collective-permute-start.6
where the time goes:
time: 742 us; the launch traced here: 733 us
  blocking collectives  534 us (72%)
  waiting for transfers between devices  93.9 us (13%)
  local copies, waits for them, and re-layouts  42.9 us (6%)
  starting transfers between devices  42.2 us (6%)
  matrix products  14.8 us (2%)
    all_gather x8, blocking collectives, body(): piece = lax.all_gather(inner, 'dp', axis=1, tiled=True)  469 us
    psum x1, blocking collectives, body(): passage_out = lax.psum(dense, 'section').astype(jnp.bfloat16)  65.4 us
    all_to_all x1, waiting for transfers between devices, body(): lax.all_to_all(outgoing, 'dp', split_axis=1, concat_axis=0, tiled=True)  62.7 us
    ppermute x7, waiting for transfers between devices, passed_along(): lax.ppermute(value, axis, [(source, source + steps) for source in range(i...  26.8 us
    ppermute x7, starting transfers between devices, passed_along(): lax.ppermute(value, axis, [(source, source + steps) for source in range(i...  15.5 us
    gather x1, local copies, waits for them, and re-layouts, body(): outgoing = jnp.take(passages, all_slots, axis=1)  15.2 us
  transfers between devices with their start and end apart: 10, of which 9 were waited for; matrix products, arithmetic and copies ran while one was open for 2% of the time, Pallas kernels for 0%

commit v1 on v0

--- a/solution.py
+++ b/solution.py
@@ -2,8 +2,14 @@
 import jax.numpy as jnp
 from jax import lax
 from jax.sharding import PartitionSpec as P
+from jax.lax import all_to_all, axis_size
 
 INVERSE_TEMP = 20.0
+
+
+def note_regions_on(u):
+    block_next = jnp.concatenate([u for _ in range(axis_size("dp"))], 1)
+    return all_to_all(block_next, "dp", 1, 1, tiled=True)
 
 
 def passed_along(value, axis, steps):
@@ -93,7 +99,7 @@
     for section_turn in range(section_count):
         active_flag = section_count - 1 - section_turn
         inner = (carry * slope).astype(jnp.bfloat16)
-        piece = lax.all_gather(inner, "dp", axis=1, tiled=True)
+        piece = note_regions_on(inner)
         back_sum = jnp.einsum("mj,ij->mi", piece, weight_rows, preferred_element_type=jnp.float32)
         weight_part = jnp.einsum("mi,mj->ij", input_cols, piece, preferred_element_type=jnp.float32)
         back_sum, layer_weight = (back_sum, weight_part)

time: 742 us -> 553 us (0.75)
  the two profiles are of different devices: /device:TPU:16 before, /device:TPU:30 now
where the time goes in v1:
time: 553 us; the launch traced here: 543 us
  blocking collectives  191 us (35%)
  waiting for transfers between devices  172 us (31%)
  local copies, waits for them, and re-layouts  89 us (16%)
  starting transfers between devices  57.2 us (10%)
  matrix products  26.2 us (5%)
    all_to_all x5, blocking collectives, note_regions_on(): return all_to_all(block_next, 'dp', 1, 1, tiled=True)  110 us
    all_to_all x1, waiting for transfers between devices, body(): lax.all_to_all(block_terms, 'dp', split_axis=0, concat_axis=1, tiled=True)  66 us
    psum x1, blocking collectives, body(): passage_out = lax.psum(dense, 'section').astype(jnp.bfloat16)  65.2 us
    all_to_all x1, waiting for transfers between devices, body(): lax.all_to_all(outgoing, 'dp', split_axis=1, concat_axis=0, tiled=True)  61 us
    unnamed x531, local copies, waits for them, and re-layouts  46.8 us
    ppermute x7, waiting for transfers between devices, passed_along(): lax.ppermute(value, axis, [(source, source + steps) for source in range(i...  29.3 us
    all_to_all x3, starting transfers between devices, note_regions_on(): return all_to_all(block_next, 'dp', 1, 1, tiled=True)  22 us
    all_to_all x1, blocking collectives, body(): lax.all_to_all(micro_cols, 'dp', split_axis=0, concat_axis=1, tiled=True)  15.4 us
  transfers between devices with their start and end apart: 12, of which 11 were waited for; matrix products, arithmetic and copies ran while one was open for 6% of the time, Pallas kernels for 0%

profile of v1, /device:TPU:30, one launch (start us, length us, event | category | flops | bytes accessed | tf_op | source)
XLA Modules:
  0.0 542.8 jit_solution(6778732099352030464)
XLA Ops:
  1.8 14.5 %gather_fusion = bf16[192,2,3584]{2,0,1:T(8,128)(2,1)} fusion(bf16[2,64,3584]{2,1,0:T(8,128)(2,1)} %param.9, s32[1024]{0:T(1024)S(1)} %pad_clamp_fusion), kind=kCustom, calls=%fused_computation | custom fusion | bytes 5505792 | tf_op jit(solution)/shard_map/jit(_take)/gather | solution.py:37
  16.4 2.1 select_bitcast_fusion
  18.5 4.4 copy.31
  22.9 14.3 %all-to-all-start = ((bf16[2,192,3584]{2,0,1:T(2,128)(2,1)}), bf16[2,192,3584]{2,0,1:T(2,128)(2,1)}, u32[]{:S(2)}, u32[]{:S(2)}) async-start(bf16[2,192,3584]{2,0,1:T(2,128)(2,1)} %copy.31), calls=%async_computation | async-start | bytes 5505024 | tf_op jit(solution)/shard_map/all_to_all | solution.py:38
  39.0 61.0 %all-to-all-done = bf16[2,192,3584]{2,0,1:T(2,128)(2,1)} async-done(((bf16[2,192,3584]{2,0,1:T(2,128)(2,1)}), bf16[2,192,3584]{2,0,1:T(2,128)(2,1)}, u32[]{:S(2)}, u32[]{:S(2)}) %all-to-all-start) | async-done | bytes 2752544 | tf_op jit(solution)/shard_map/all_to_all | solution.py:38
  99.9 5.2 copy.32
  105.2 6.8 %reshape.419 = bf16[128,3,3584]{2,0,1:T(8,128)(2,1)} reshape(bf16[64,2,3,3584]{3,1,0,2:T(2,128)(2,1)} %copy.32) | data formatting | bytes 5505024 | tf_op jit(solution)/shard_map/reshape.6
  111.9 2.8 fusion.27
  115.1 1.6 fusion.58
  116.8 15.4 %all_to_all.135 = f32[64,1,56]{2,1,0:T(1,128)S(1)} all-to-all(f32[64,1,56]{2,1,0:T(1,128)S(1)} %bitcast.260), channel_id=1, replica_groups=mesh['section'=8,'dp'=64] {'dp'}, dimensions={0} | all-to-all | bytes 28672 | tf_op jit(solution)/shard_map/all_to_all | solution.py:77
  133.0 21.1 %all_to_all.136 = bf16[64,2,1792]{2,1,0:T(2,128)(2,1)S(1)} all-to-all(bf16[64,2,1792]{2,1,0:T(2,128)(2,1)S(1)} %reshape.438), channel_id=1, replica_groups=mesh['section'=8,'dp'=64] {'dp'}, dimensions={0} | all-to-all | bytes 917504 | tf_op jit(solution)/shard_map/all_to_all | solution.py:12
  155.0 2.4 collective-permute-start
  157.4 4.6 collective-permute-done
  163.8 2.2 reshape.440
  166.0 22.2 %all_to_all.137 = bf16[64,2,1792]{2,1,0:T(2,128)(2,1)S(1)} all-to-all(bf16[64,2,1792]{2,1,0:T(2,128)(2,1)S(1)} %reshape.440), channel_id=1, replica_groups=mesh['section'=8,'dp'=64] {'dp'}, dimensions={0} | all-to-all | bytes 917504 | tf_op jit(solution)/shard_map/all_to_all | solution.py:12
  189.1 1.9 collective-permute-start.1
  191.0 5.0 collective-permute-done.1
  197.8 2.2 reshape.442
  200.0 22.1 %all_to_all.138 = bf16[64,2,1792]{2,1,0:T(2,128)(2,1)} all-to-all(bf16[64,2,1792]{2,1,0:T(2,128)(2,1)S(1)} %reshape.442), channel_id=1, replica_groups=mesh['section'=8,'dp'=64] {'dp'}, dimensions={0} | all-to-all | bytes 917504 | tf_op jit(solution)/shard_map/all_to_all | solution.py:12
  222.2 2.1 reshape.443
  224.6 1.9 collective-permute-start.2
  226.5 5.0 collective-permute-done.2
  233.3 2.8 reshape.444
  236.2 22.3 %all_to_all.139 = bf16[64,2,1792]{2,1,0:T(2,128)(2,1)} all-to-all(bf16[64,2,1792]{2,1,0:T(2,128)(2,1)} %reshape.444), channel_id=1, replica_groups=mesh['section'=8,'dp'=64] {'dp'}, dimensions={0} | all-to-all | bytes 917504 | tf_op jit(solution)/shard_map/all_to_all | solution.py:12
  258.5 2.8 reshape.445
  261.2 1.4 convolution_add_fusion.4
  262.7 1.9 collective-permute-start.3
  264.6 5.0 collective-permute-done.3
  271.5 2.8 reshape.446
  274.3 22.7 %all_to_all.140 = bf16[64,2,1792]{2,1,0:T(2,128)(2,1)} all-to-all(bf16[64,2,1792]{2,1,0:T(2,128)(2,1)} %reshape.446), channel_id=1, replica_groups=mesh['section'=8,'dp'=64] {'dp'}, dimensions={0} | all-to-all | bytes 917504 | tf_op jit(solution)/shard_map/all_to_all | solution.py:12
  297.0 2.8 reshape.447
  299.8 1.4 convolution_add_fusion.3
  301.2 1.9 collective-permute-start.4
  303.2 5.0 collective-permute-done.4
  309.1 0.9 copy-done.11
  310.0 2.8 reshape.448
  312.9 7.0 %all-to-all-start.8 = ((bf16[64,2,1792]{2,1,0:T(2,128)(2,1)}), bf16[64,2,1792]{2,1,0:T(2,128)(2,1)}, u32[]{:S(2)}, u32[]{:S(2)}) async-start(bf16[64,2,1792]{2,1,0:T(2,128)(2,1)} %reshape.448), calls=%async_computation.8 | async-start | bytes 917504 | tf_op jit(solution)/shard_map/all_to_all | solution.py:12
  320.7 4.1 copy.35
  324.9 10.3 %all-to-all-done.8 = bf16[64,2,1792]{2,1,0:T(2,128)(2,1)} async-done(((bf16[64,2,1792]{2,1,0:T(2,128)(2,1)}), bf16[64,2,1792]{2,1,0:T(2,128)(2,1)}, u32[]{:S(2)}, u32[]{:S(2)}) %all-to-all-start.8) | async-done | bytes 458784 | tf_op jit(solution)/shard_map/all_to_all | solution.py:12
  335.2 7.0 %all-to-all-start.1 = ((bf16[128,3,3584]{2,1,0:T(4,128)(2,1)}), bf16[128,3,3584]{2,1,0:T(4,128)(2,1)}, u32[]{:S(2)}, u32[]{:S(2)}) async-start(bf16[128,3,3584]{2,1,0:T(4,128)(2,1)} %copy.35), calls=%async_computation.1 | async-start | bytes 7340032 | tf_op jit(solution)/shard_map/all_to_all | solution.py:76
  342.2 2.8 reshape.449
  345.0 1.4 convolution_add_fusion.2
  346.4 1.9 collective-permute-start.5
  348.3 1.8 convolution_select_fusion
  350.2 3.2 collective-permute-done.5
  355.0 1.0 copy-done.12
  356.0 2.8 reshape.450
  358.8 66.0 %all-to-all-done.1 = bf16[128,3,3584]{2,1,0:T(4,128)(2,1)} async-done(((bf16[128,3,3584]{2,1,0:T(4,128)(2,1)}), bf16[128,3,3584]{2,1,0:T(4,128)(2,1)}, u32[]{:S(2)}, u32[]{:S(2)}) %all-to-all-start.1) | async-done | bytes 2752544 | tf_op jit(solution)/shard_map/all_to_all | solution.py:76
  424.9 8.1 %all-to-all-start.9 = ((bf16[64,2,1792]{2,1,0:T(2,128)(2,1)}), bf16[64,2,1792]{2,1,0:T(2,128)(2,1)}, u32[]{:S(2)}, u32[]{:S(2)}) async-start(bf16[64,2,1792]{2,1,0:T(2,128)(2,1)} %reshape.450), calls=%async_computation.9 | async-start | bytes 917504 | tf_op jit(solution)/shard_map/all_to_all | solution.py:12
  433.0 1.5 convolution_select_fusion.1
  434.5 1.4 convolution_select_fusion.2
  437.2 6.0 %copy.36 = bf16[64,2,3,3584]{3,1,2,0:T(2,128)(2,1)} copy(bf16[64,2,3,3584]{3,2,1,0:T(4,128)(2,1)} %bitcast.19) | data formatting | bytes 5505024 | tf_op jit(solution)/shard_map/all_to_all | solution.py:76
  443.2 5.1 all-to-all-done.9
  448.3 2.1 reshape.451
  450.7 1.9 collective-permute-start.6
  452.6 3.7 convolution_bitcast_fusion
  456.3 1.4 collective-permute-done.6
  459.5 2.9 reshape.452
  462.3 7.0 %all-to-all-start.10 = ((bf16[64,2,1792]{2,1,0:T(2,128)(2,1)}), bf16[64,2,1792]{2,1,0:T(2,128)(2,1)}, u32[]{:S(2)}, u32[]{:S(2)}) async-start(bf16[64,2,1792]{2,1,0:T(2,128)(2,1)} %reshape.452), calls=%async_computation.10 | async-start | bytes 917504 | tf_op jit(solution)/shard_map/all_to_all | solution.py:12
  469.3 65.2 %all-reduce.1 = bf16[2,64,3584]{2,1,0:T(8,128)(2,1)} all-reduce(f32[2,64,3584]{2,1,0:T(8,128)} %convolution_bitcast_fusion), channel_id=1, replica_groups=mesh['section'=8,'dp'=64] {'section'}, use_global_device_ids=true, to_apply=%region_4.5 | all-reduce | flops 458752 | bytes 2752512 | tf_op jit(solution)/shard_map/psum | solution.py:88
  534.5 1.4 convolution_select_fusion.5
  535.9 1.4 convolution_select_fusion.6
  537.4 2.1 reshape.453
  539.5 2.1 fusion.4
  (555 shorter events, 19.2 us)
Async XLA Ops:
  0.6 111.3 %copy-start = (bf16[128,3584]{1,0:T(8,128)(2,1)S(1)}, bf16[128,3584]{1,0:T(8,128)(2,1)}, u32[]{:S(2)}) copy-start(bf16[128,3584]{1,0:T(8,128)(2,1)} %param.8) | copy-start | bytes 2752516
  1.6 14.7 %copy-start.36 = (s32[192]{0:T(256)}, s32[192]{0:T(256)S(1)}, u32[]{:S(2)}) copy-start(s32[192]{0:T(256)S(1)} %reshape.417) | copy-start | bytes 2308
  22.9 14.3 %copy-start.17 = (f32[128,384]{1,0:T(8,128)S(1)}, f32[128,384]{1,0:T(8,128)}, u32[]{:S(2)}) copy-start(f32[128,384]{1,0:T(8,128)} %param.12) | copy-start | bytes 589828
  22.9 14.5 %copy-start.38 = (s32[64]{0:T(128)S(1)}, s32[64]{0:T(128)}, u32[]{:S(2)}) copy-start(s32[64]{0:T(128)} %param.11) | copy-start | bytes 772
  22.9 77.0 %all-to-all-start = ((bf16[2,192,3584]{2,0,1:T(2,128)(2,1)}), bf16[2,192,3584]{2,0,1:T(2,128)(2,1)}, u32[]{:S(2)}, u32[]{:S(2)}) async-start(bf16[2,192,3584]{2,0,1:T(2,128)(2,1)} %copy.31), calls=%async_computation | async-start | bytes 5505024 | tf_op jit(solution)/shard_map/all_to_all | solution.py:38
  111.9 3.1 copy-start.1
  115.1 17.2 %copy-start.15 = (bf16[1,64,56]{1,2,0:T(8,128)(2,1)S(1)}, bf16[1,64,56]{1,2,0:T(8,128)(2,1)}, u32[]{:S(2)}) copy-start(bf16[1,64,56]{1,2,0:T(8,128)(2,1)} %param.15) | copy-start | bytes 21508
  116.7 38.0 %copy-start.2 = (bf16[1,56,3584]{2,1,0:T(8,128)(2,1)S(1)}, bf16[1,56,3584]{2,1,0:T(8,128)(2,1)}, u32[]{:S(2)}) copy-start(bf16[1,56,3584]{2,1,0:T(8,128)(2,1)} %param.13) | copy-start | bytes 1204228
  154.7 11.3 %copy-start.6 = (bf16[64,56,64]{2,1,0:T(8,128)(2,1)}, bf16[64,56,64]{2,1,0:T(8,128)(2,1)S(1)}, u32[]{:S(2)}) copy-start(bf16[64,56,64]{2,1,0:T(8,128)(2,1)S(1)} %reshape.439) | copy-start | bytes 1376260
  155.0 2.4 copy-start.22
  155.0 7.0 %collective-permute-start = (f32[64,56]{0,1:T(8,128)S(1)}, f32[64,56]{0,1:T(8,128)S(1)}, u32[]{:S(2)}, u32[]{:S(2)}) collective-permute-start(f32[64,56]{0,1:T(8,128)S(1)} %convolution_add_fusion.7), channel_id=1, source_target_pairs={{64,0},{128,64},{192,128},{256,192},{320,256},{384,320},{448,384},... | collective-permute-start | bytes 43016 | tf_op jit(solution)/shard_map/ppermute | solution.py:18
  162.9 0.9 copy-start.7
  189.1 1.9 copy-start.24
  189.1 7.0 %collective-permute-start.1 = (f32[64,56]{0,1:T(8,128)S(1)}, f32[64,56]{0,1:T(8,128)S(1)}, u32[]{:S(2)}, u32[]{:S(2)}) collective-permute-start(f32[64,56]{0,1:T(8,128)S(1)} %convolution_add_fusion.6), channel_id=1, source_target_pairs={{64,0},{128,64},{192,128},{256,192},{320,256},{384,320},{448,384},... | collective-permute-start | bytes 43016 | tf_op jit(solution)/shard_map/ppermute | solution.py:18
  196.9 0.9 copy-start.8
  224.5 8.8 %copy-start.26 = (f32[64,56]{0,1:T(8,128)}, f32[64,56]{0,1:T(8,128)S(1)}, u32[]{:S(2)}) copy-start(f32[64,56]{0,1:T(8,128)S(1)} %convolution_add_fusion.5) | copy-start | bytes 43012
  224.6 7.0 %collective-permute-start.2 = (f32[64,56]{0,1:T(8,128)S(1)}, f32[64,56]{0,1:T(8,128)S(1)}, u32[]{:S(2)}, u32[]{:S(2)}) collective-permute-start(f32[64,56]{0,1:T(8,128)S(1)} %convolution_add_fusion.5), channel_id=1, source_target_pairs={{64,0},{128,64},{192,128},{256,192},{320,256},{384,320},{448,384},... | collective-permute-start | bytes 43016 | tf_op jit(solution)/shard_map/ppermute | solution.py:18
  232.4 0.9 copy-start.9
  262.7 8.8 %copy-start.28 = (f32[64,56]{0,1:T(8,128)}, f32[64,56]{0,1:T(8,128)S(1)}, u32[]{:S(2)}) copy-start(f32[64,56]{0,1:T(8,128)S(1)} %convolution_add_fusion.4) | copy-start | bytes 43012
  262.7 7.0 %collective-permute-start.3 = (f32[64,56]{0,1:T(8,128)S(1)}, f32[64,56]{0,1:T(8,128)S(1)}, u32[]{:S(2)}, u32[]{:S(2)}) collective-permute-start(f32[64,56]{0,1:T(8,128)S(1)} %convolution_add_fusion.4), channel_id=1, source_target_pairs={{64,0},{128,64},{192,128},{256,192},{320,256},{384,320},{448,384},... | collective-permute-start | bytes 43016 | tf_op jit(solution)/shard_map/ppermute | solution.py:18
  270.5 0.9 copy-start.10
  301.2 8.8 %copy-start.30 = (f32[64,56]{0,1:T(8,128)}, f32[64,56]{0,1:T(8,128)S(1)}, u32[]{:S(2)}) copy-start(f32[64,56]{0,1:T(8,128)S(1)} %convolution_add_fusion.3) | copy-start | bytes 43012
  301.2 7.0 %collective-permute-start.4 = (f32[64,56]{0,1:T(8,128)S(1)}, f32[64,56]{0,1:T(8,128)S(1)}, u32[]{:S(2)}, u32[]{:S(2)}) collective-permute-start(f32[64,56]{0,1:T(8,128)S(1)} %convolution_add_fusion.3), channel_id=1, source_target_pairs={{64,0},{128,64},{192,128},{256,192},{320,256},{384,320},{448,384},... | collective-permute-start | bytes 43016 | tf_op jit(solution)/shard_map/ppermute | solution.py:18
  309.1 1.0 copy-start.11
  312.9 22.3 %all-to-all-start.8 = ((bf16[64,2,1792]{2,1,0:T(2,128)(2,1)}), bf16[64,2,1792]{2,1,0:T(2,128)(2,1)}, u32[]{:S(2)}, u32[]{:S(2)}) async-start(bf16[64,2,1792]{2,1,0:T(2,128)(2,1)} %reshape.448), calls=%async_computation.8 | async-start | bytes 917504 | tf_op jit(solution)/shard_map/all_to_all | solution.py:12
  335.2 89.6 %all-to-all-start.1 = ((bf16[128,3,3584]{2,1,0:T(4,128)(2,1)}), bf16[128,3,3584]{2,1,0:T(4,128)(2,1)}, u32[]{:S(2)}, u32[]{:S(2)}) async-start(bf16[128,3,3584]{2,1,0:T(4,128)(2,1)} %copy.35), calls=%async_computation.1 | async-start | bytes 7340032 | tf_op jit(solution)/shard_map/all_to_all | solution.py:76
  346.4 9.6 %copy-start.32 = (f32[64,56]{0,1:T(8,128)}, f32[64,56]{0,1:T(8,128)S(1)}, u32[]{:S(2)}) copy-start(f32[64,56]{0,1:T(8,128)S(1)} %convolution_add_fusion.2) | copy-start | bytes 43012
  346.4 7.0 %collective-permute-start.5 = (f32[64,56]{0,1:T(8,128)S(1)}, f32[64,56]{0,1:T(8,128)S(1)}, u32[]{:S(2)}, u32[]{:S(2)}) collective-permute-start(f32[64,56]{0,1:T(8,128)S(1)} %convolution_add_fusion.2), channel_id=1, source_target_pairs={{64,0},{128,64},{192,128},{256,192},{320,256},{384,320},{448,384},... | collective-permute-start | bytes 43016 | tf_op jit(solution)/shard_map/ppermute | solution.py:18
  353.4 2.6 copy-start.20
  355.0 1.0 copy-start.12
  424.9 23.4 %all-to-all-start.9 = ((bf16[64,2,1792]{2,1,0:T(2,128)(2,1)}), bf16[64,2,1792]{2,1,0:T(2,128)(2,1)}, u32[]{:S(2)}, u32[]{:S(2)}) async-start(bf16[64,2,1792]{2,1,0:T(2,128)(2,1)} %reshape.450), calls=%async_computation.9 | async-start | bytes 917504 | tf_op jit(solution)/shard_map/all_to_all | solution.py:12
  432.9 2.9 copy-start.3
  433.0 2.9 copy-start.14
  433.0 3.6 copy-start.4
  437.2 13.1 %copy-start.21 = (f32[64,56]{0,1:T(8,128)S(1)}, f32[64,56]{0,1:T(8,128)}, u32[]{:S(2)}) copy-start(f32[64,56]{0,1:T(8,128)} %copy-done.20) | copy-start | bytes 43012
  443.2 9.4 %copy-start.37 = (s32[192]{0:T(256)S(1)}, s32[192]{0:T(256)}, u32[]{:S(2)}) copy-start(s32[192]{0:T(256)} %copy-done.36) | copy-start | bytes 2308
  450.4 7.3 %copy-start.16 = (bf16[1,64,56]{1,2,0:T(8,128)(2,1)S(1)}, bf16[1,64,56]{1,2,0:T(8,128)(2,1)}, u32[]{:S(2)}) copy-start(bf16[1,64,56]{1,2,0:T(8,128)(2,1)} %param.15) | copy-start | bytes 21508
  450.7 7.4 %copy-start.34 = (f32[64,56]{0,1:T(8,128)}, f32[64,56]{0,1:T(8,128)S(1)}, u32[]{:S(2)}) copy-start(f32[64,56]{0,1:T(8,128)S(1)} %convolution_add_fusion.1) | copy-start | bytes 43012
  450.7 7.0 %collective-permute-start.6 = (f32[64,56]{0,1:T(8,128)S(1)}, f32[64,56]{0,1:T(8,128)S(1)}, u32[]{:S(2)}, u32[]{:S(2)}) collective-permute-start(f32[64,56]{0,1:T(8,128)S(1)} %convolution_add_fusion.1), channel_id=1, source_target_pairs={{64,0},{128,64},{192,128},{256,192},{320,256},{384,320},{448,384},... | collective-permute-start | bytes 43016 | tf_op jit(solution)/shard_map/ppermute | solution.py:18
  457.7 1.8 copy-start.18
  458.3 76.2 %copy-start.5 = (bf16[64,56,64]{2,1,0:T(8,128)(2,1)S(1)}, bf16[64,56,64]{2,1,0:T(8,128)(2,1)}, u32[]{:S(2)}) copy-start(bf16[64,56,64]{2,1,0:T(8,128)(2,1)} %reshape.449) | copy-start | bytes 1376260
  458.6 0.9 copy-start.13
  462.3 75.0 %all-to-all-start.10 = ((bf16[64,2,1792]{2,1,0:T(2,128)(2,1)}), bf16[64,2,1792]{2,1,0:T(2,128)(2,1)}, u32[]{:S(2)}, u32[]{:S(2)}) async-start(bf16[64,2,1792]{2,1,0:T(2,128)(2,1)} %reshape.452), calls=%async_computation.10 | async-start | bytes 917504 | tf_op jit(solution)/shard_map/all_to_all | solution.py:12
  537.3 4.3 copy-start.19
  537.3 4.3 copy-start.23
  537.3 4.3 copy-start.25
  537.3 4.3 copy-start.27
  537.3 4.3 copy-start.29
  537.3 4.3 copy-start.31
  537.3 4.3 copy-start.33
  537.3 4.3 copy-start.35
